TPU v7x, 256 devices: a whole 4x4x8 slice. The times are simulated.
256 devices in a mesh: section: 2 (over core), seq: 16 (over x, y), exp: 8 (over z).
Axes of the slice: x: 4, y: 4, z: 8, core: 2. Of those that a mesh axis runs over, the one named last changes fastest.
Arguments:
- hidden_in: bfloat16 [2048, 2048], P('seq'), may hold values from -6 to 6
- seg_ids: int32 [2048], P('seq'), may hold values from 0 to 7, never falling along the last dimension, each value on 1 to 1024 neighbouring positions
- attn_gain: float32 [2048], replicated, may hold values from 0.25 to 1.75
- w_query: bfloat16 [2048, 2048], P(None, ('section', 'exp'))
- w_key: bfloat16 [2048, 2048], P(None, ('section', 'exp'))
- w_value: bfloat16 [2048, 2048], P(None, ('section', 'exp')), may hold values from -0.125 to 0.125
- w_out: bfloat16 [2048, 2048], P(('section', 'exp')), may hold values from -0.5 to 0.5
- moe_gain: float32 [2048], replicated, may hold values from 0.25 to 1.75
- expert_ids: int32 [2048, 8], P(('seq', 'exp')), may hold values from 0 to 63, all different within a row; in each aligned block of 16 rows (0 to 15, 16 to 31, ...) at most 4 rows name the same one
- route_weights: float32 [2048, 8], P(('seq', 'exp')), may hold values from 0.1 to 0.6
- gate_halves: bfloat16 [128, 2048, 512], P(('seq', 'exp'), None, 'section'), may hold values from -0.125 to 0.125
- up_halves: bfloat16 [128, 2048, 512], P(('seq', 'exp'), None, 'section'), may hold values from -0.125 to 0.125
- down_halves: bfloat16 [128, 512, 2048], P(('seq', 'exp'), 'section'), may hold values from -0.1875 to 0.1875
Outputs:
- layer_out: bfloat16 [2048, 2048], P(('seq', 'exp'))
Inputs may be any that keep to these rules, and one draw needn't show every extreme that they name: `seg_ids`: prompt numbers never fall along the batch; each prompt holds 1 to 1024 tokens, and one holds exactly 1024. `expert_ids`: A token's 8 experts are distinct. In each aligned block of 16 tokens (the tokens of one device along seq and exp), no expert is chosen by more than 4 of the block's tokens, a bound that some block reaches.
All inputs are finite; a program needn't handle non-finite values.
Results may differ from a plain program's by a relative error of at most 0.012.
Values may be sent and summed in bfloat16 or wider, within the bound.
No kernel may reach another device: no remote copies, remote signals or barrier semaphores. Data moves between devices by JAX's collectives and lax.ppermute only.
A program may use at most 64 MiB of HBM per device.

v0:
```python
import math
import jax
import jax.numpy as jnp
from jax import lax
from jax.sharding import PartitionSpec as P

epsilon = 1e-05
rope_base = 10000.0


def rms_scale(rows, gain):
    wide = rows.astype(jnp.float32)
    inverse = lax.rsqrt(jnp.mean(wide * wide, axis=-1, keepdims=True) + epsilon)
    return (wide * inverse * gain).astype(jnp.bfloat16)


def rotate(values, positions):
    half_dim = values.shape[-1] // 2
    frequency = rope_base ** (-2.0 * jnp.arange(half_dim, dtype=jnp.float32) / values.shape[-1])
    angles = positions.astype(jnp.float32)[:, None] * frequency[None, :]
    cosine = jnp.cos(angles)
    sine_part = jnp.sin(angles)
    first_half = values[:, :half_dim]
    second_half = values[:, half_dim:]
    return jnp.concatenate(
        [
            first_half * cosine - second_half * sine_part,
            second_half * cosine + first_half * sine_part,
        ],
        axis=-1,
    )


def per_device(
    hidden_in,
    seg_ids,
    attn_gain,
    w_query,
    w_key,
    w_value,
    w_out,
    moe_gain,
    expert_ids,
    route_weights,
    gate_halves,
    up_halves,
    down_halves,
):
    tok_seq = hidden_in.shape[0]
    width = hidden_in.shape[1]
    head_dim = w_query.shape[1]
    positions = lax.axis_index("seq") * tok_seq + jnp.arange(tok_seq, dtype=jnp.int32)
    normed = rms_scale(hidden_in, attn_gain)
    query_rows = rotate(
        jnp.dot(normed, w_query, preferred_element_type=jnp.float32), positions
    ).astype(jnp.bfloat16)
    key_rows = rotate(jnp.dot(normed, w_key, preferred_element_type=jnp.float32), positions).astype(
        jnp.bfloat16
    )
    value_rows = jnp.dot(normed, w_value, preferred_element_type=jnp.float32).astype(jnp.bfloat16)
    score_scale = 1.0 / math.sqrt(head_dim)
    run_max = jnp.full((tok_seq,), -1e30, jnp.float32)
    piece_keys = lax.all_gather(key_rows, "seq", axis=0, tiled=True)
    piece_values = lax.all_gather(value_rows, "seq", axis=0, tiled=True)
    key_segs = lax.all_gather(seg_ids, "seq", axis=0, tiled=True)
    piece_rows = piece_keys.shape[0]
    scores = (
        lax.dot_general(
            query_rows, piece_keys, (((1,), (1,)), ((), ())), preferred_element_type=jnp.float32
        )
        * score_scale
    )
    key_pos = jnp.arange(piece_rows, dtype=jnp.int32)
    allowed = (seg_ids[:, None] == key_segs[None, :]) & (key_pos[None, :] <= positions[:, None])
    masked = jnp.where(allowed, scores, -1e30)
    new_max = jnp.maximum(run_max, jnp.max(masked, axis=1))
    weights = jnp.where(allowed, jnp.exp(masked - new_max[:, None]), 0.0)
    run_total = jnp.sum(weights, axis=1)
    weighted_sum = jnp.dot(
        weights.astype(jnp.bfloat16), piece_values, preferred_element_type=jnp.float32
    )
    run_max, run_total, weighted_sum = (new_max, run_total, weighted_sum)
    head_out = (weighted_sum / run_total[:, None]).astype(jnp.bfloat16)
    partial_value = jnp.dot(head_out, w_out, preferred_element_type=jnp.float32)
    tok_dev = tok_seq // lax.axis_size("exp")
    own_start = lax.axis_index("exp") * tok_dev
    summed = lax.psum(partial_value, ("section", "exp"))
    summed = lax.dynamic_slice_in_dim(summed, own_start, tok_dev, 0)
    own_rows = lax.dynamic_slice_in_dim(hidden_in, own_start, tok_dev, 0)
    residual = (own_rows.astype(jnp.float32) + summed).astype(jnp.bfloat16)
    moe_in = rms_scale(residual, moe_gain)
    experts = lax.axis_size("seq") * lax.axis_size("exp") // 2
    top_count = expert_ids.shape[1]
    capacity = min(tok_dev, max(2, 2 * tok_dev * top_count // experts))
    row_count = tok_dev * top_count
    flat_ids = expert_ids.reshape(row_count)
    one_hot = (flat_ids[:, None] == jnp.arange(experts, dtype=jnp.int32)[None, :]).astype(jnp.int32)
    slot_rank = jnp.sum((jnp.cumsum(one_hot, axis=0) - one_hot) * one_hot, axis=1)
    slot_index = flat_ids * capacity + slot_rank
    placed = slot_index[:, None] == jnp.arange(experts * capacity, dtype=jnp.int32)[None, :]
    repeated = jnp.repeat(moe_in, top_count, axis=0)
    outgoing = lax.dot_general(
        placed.astype(jnp.bfloat16),
        repeated,
        (((0,), (0,)), ((), ())),
        preferred_element_type=jnp.float32,
    ).astype(jnp.bfloat16)
    row_token = jnp.arange(row_count, dtype=jnp.int32) // top_count
    token_hot = (row_token[None, :] == jnp.arange(tok_dev, dtype=jnp.int32)[:, None]).astype(
        jnp.float32
    )
    weighted = token_hot * route_weights.reshape(row_count)[None, :]
    combine = jnp.dot(weighted, placed.astype(jnp.float32), precision=lax.Precision.HIGHEST)
    doubled = jnp.broadcast_to(
        outgoing.reshape(experts, 1, capacity, width), (experts, 2, capacity, width)
    ).reshape(2 * experts, capacity, width)
    arrived = lax.all_to_all(doubled, ("seq", "exp"), split_axis=0, concat_axis=0, tiled=True)
    flat_rows = arrived.reshape(-1, width)
    gate_proj = jnp.dot(flat_rows, gate_halves[0], preferred_element_type=jnp.float32)
    up_proj = jnp.dot(flat_rows, up_halves[0], preferred_element_type=jnp.float32)
    activated = (jax.nn.silu(gate_proj) * up_proj).astype(jnp.bfloat16)
    returned = lax.all_to_all(
        jnp.dot(activated, down_halves[0], preferred_element_type=jnp.float32)
        .astype(jnp.bfloat16)
        .reshape(arrived.shape),
        ("seq", "exp"),
        split_axis=0,
        concat_axis=0,
        tiled=True,
    )
    halves_sum = jnp.sum(
        returned.reshape(experts, 2, capacity, width).astype(jnp.float32), axis=1
    ).reshape(experts * capacity, width)
    moe_part = jnp.dot(combine, halves_sum, precision=lax.Precision.HIGHEST)
    moe_total = lax.psum(moe_part, "section")
    return (residual.astype(jnp.float32) + moe_total).astype(jnp.bfloat16)


def solution(mesh):
    in_specs = (
        P("seq", None),
        P("seq"),
        P(),
        P(None, ("section", "exp")),
        P(None, ("section", "exp")),
        P(None, ("section", "exp")),
        P(("section", "exp"), None),
        P(),
        P(("seq", "exp"), None),
        P(("seq", "exp"), None),
        P(("seq", "exp"), None, "section"),
        P(("seq", "exp"), None, "section"),
        P(("seq", "exp"), "section", None),
    )
    out_specs = P(("seq", "exp"), None)
    return jax.shard_map(
        per_device, mesh=mesh, in_specs=in_specs, out_specs=out_specs, check_vma=False
    )
```

profile of v0, /device:TPU:1, one launch (start us, length us, event | category | flops | bytes accessed | tf_op | source)
XLA Modules:
  0.0 376.0 jit_solution(10940934380651629049)
XLA Ops:
  6.5 0.0 copy-start
  6.5 0.0 all-reduce.3.cloned.1.call-start
  6.6 1.3 fusion.4
  7.9 1.6 fusion.74
  9.5 0.0 copy-start.2
  9.5 0.0 copy-start.7
  9.6 0.0 copy-start.8
  9.6 1.7 fusion.76
  11.3 0.2 fusion.52
  11.5 20.5 %all_gather.10 = bf16[2048,128]{0,1:T(8,128)(2,1)S(1)} all-gather(bf16[128,128]{0,1:T(8,128)(2,1)S(1)} %pad_maximum_fusion), channel_id=1, replica_groups=mesh['section'=2,'seq'=16,'exp'=8] {'seq'}, dimensions={0}, use_global_device_ids=true | all-gather | bytes 557056 | tf_op jit(solution)/shard_map/all_gather | solution.py:63
  32.0 15.7 %all-gather = s32[16,1,128]{2,1,0:T(1,128)S(1)} all-gather(s32[1,1,128]{2,1,0:T(1,128)S(1)} %bitcast.33), channel_id=1, replica_groups=mesh['section'=2,'seq'=16,'exp'=8] {'seq'}, dimensions={0}, use_global_device_ids=true | all-gather | bytes 8704 | tf_op jit(solution)/shard_map/all_gather | solution.py:65
  47.8 0.5 fusion.78
  48.3 0.4 convolution_convert_fusion.2
  48.7 16.1 %all_gather.11 = bf16[2048,128]{1,0:T(8,128)(2,1)S(1)} all-gather(bf16[128,128]{1,0:T(8,128)(2,1)S(1)} %convolution_convert_fusion.2), channel_id=1, replica_groups=mesh['section'=2,'seq'=16,'exp'=8] {'seq'}, dimensions={0}, use_global_device_ids=true | all-gather | bytes 557056 | tf_op jit(solution)/shard_map/all_gather | solution.py:64
  64.8 0.4 fusion.13
  65.2 0.0 copy-start.3
  65.2 2.8 fusion.3
  68.0 0.0 all-reduce.3.cloned.1.call-update
  68.1 0.1 copy.19
  68.1 0.1 reshape.82
  68.2 0.1 fusion.42
  68.3 0.2 reduce_window_sum.11
  68.5 0.2 select_reduce_fusion
  68.7 128.0 %all-reduce.3.cloned.1.call-done = f32[128,2048]{1,0:T(8,128)} async-done(((f32[128,2048]{1,0:T(8,128)}), f32[128,2048]{1,0:T(8,128)}) %all-reduce.3.cloned.1.call-update) | async-done | bytes 1048592 | tf_op jit(solution)/shard_map/psum | solution.py:87
  196.7 1.0 fusion.35
  197.7 0.1 fusion.37
  197.8 0.5 convolution_convert_fusion.1
  198.4 0.4 broadcast_in_dim.19
  198.8 1.2 broadcast_in_dim.20
  200.1 63.0 %all_to_all.10 = bf16[128,4,2048]{2,1,0:T(4,128)(2,1)S(1)} all-to-all(bf16[128,4,2048]{2,1,0:T(4,128)(2,1)S(1)} %bitcast.29), channel_id=1, replica_groups=mesh['section'=2,'seq'=16,'exp'=8] {'seq','exp'}, dimensions={0} | all-to-all | bytes 4194304 | tf_op jit(solution)/shard_map/all_to_all | solution.py:117
  263.1 2.1 reshape.85
  265.1 3.5 fusion.10
  268.7 0.0 copy-done
  268.7 5.0 %convolution_convert_fusion = bf16[512,2048]{1,0:T(8,128)(2,1)} fusion(bf16[512,2048]{1,0:T(8,128)(2,1)S(1)} %copy-done.1, bf16[1,256,2048]{2,1,0:T(8,128)(2,1)S(1)} %copy-done, bf16[1,2048,256]{2,1,0:T(8,128)(2,1)} %param.24, f32[512,256]{1,0:T(8,128)} %fusion.10), kind=kOutput, calls=%fused_computation.1 | convolution fusion | flops 1075576832 | bytes 6815744 | tf_op jit(solution)/shard_map/dot_general | solution.py:123
  273.7 4.1 %reshape.86 = bf16[128,4,2048]{2,1,0:T(4,128)(2,1)} reshape(bf16[512,2048]{1,0:T(8,128)(2,1)} %convolution_convert_fusion) | data formatting | bytes 4194304 | tf_op jit(solution)/shard_map/reshape | solution.py:125
  277.8 6.7 %all-to-all-start.1 = ((bf16[128,4,2048]{2,1,0:T(4,128)(2,1)}), bf16[128,4,2048]{2,1,0:T(4,128)(2,1)S(1)}, u32[]{:S(2)}, u32[]{:S(2)}) async-start(bf16[128,4,2048]{2,1,0:T(4,128)(2,1)} %reshape.86), calls=%async_computation.1 | async-start | bytes 4194304 | tf_op jit(solution)/shard_map/all_to_all | solution.py:122
  284.6 0.2 all-reduce.5.cloned.1.call-start
  284.8 0.0 copy-done.6
  284.8 0.1 copy.18
  284.9 0.1 mul.147
  285.0 0.2 fusion.39
  285.2 49.4 %all-to-all-done.1 = bf16[128,4,2048]{2,1,0:T(4,128)(2,1)S(1)} async-done(((bf16[128,4,2048]{2,1,0:T(4,128)(2,1)}), bf16[128,4,2048]{2,1,0:T(4,128)(2,1)S(1)}, u32[]{:S(2)}, u32[]{:S(2)}) %all-to-all-start.1) | async-done | bytes 2097184 | tf_op jit(solution)/shard_map/all_to_all | solution.py:122
  334.5 2.7 convert_reduce_fusion
  337.2 2.0 reshape.87
  339.2 1.8 fusion.79
  341.0 0.0 all-reduce.5.cloned.1.call-update
  341.0 26.6 %all-reduce.5.cloned.1.call-done = f32[16,2048]{1,0:T(8,128)} async-done(((f32[16,2048]{1,0:T(8,128)}), f32[16,2048]{1,0:T(8,128)}) %all-reduce.5.cloned.1.call-update) | async-done | bytes 131088 | tf_op jit(solution)/shard_map/psum | solution.py:135
  367.6 1.5 fusion.38
  (20 shorter events, 0.1 us)
Async XLA Ops:
  6.5 262.1 %copy-start = (bf16[1,256,2048]{2,1,0:T(8,128)(2,1)S(1)}, bf16[1,256,2048]{2,1,0:T(8,128)(2,1)}, u32[]{:S(2)}) copy-start(bf16[1,256,2048]{2,1,0:T(8,128)(2,1)} %param.25) | copy-start | bytes 3145732
  6.5 25.5 %copy-start.4 = (s32[128]{0:T(128)S(1)}, s32[128]{0:T(128)}, u32[]{:S(2)}) copy-start(s32[128]{0:T(128)} %param.14) | copy-start | bytes 1540
  6.5 190.1 %all-reduce.3.cloned.1.call-start = ((), (), s32[]{:S(2)}) async-start(), calls=%async_computation.2 | async-start | bytes 2097152 | tf_op jit(solution)/shard_map/psum | solution.py:87
  9.5 38.8 %copy-start.2 = (bf16[128,2048]{1,0:T(8,128)(2,1)S(1)}, bf16[128,2048]{1,0:T(8,128)(2,1)}, u32[]{:S(2)}) copy-start(bf16[128,2048]{1,0:T(8,128)(2,1)} %param.13) | copy-start | bytes 1572868
  9.5 38.8 %copy-start.7 = (bf16[2048,128]{1,0:T(8,128)(2,1)S(1)}, bf16[2048,128]{1,0:T(8,128)(2,1)}, u32[]{:S(2)}) copy-start(bf16[2048,128]{1,0:T(8,128)(2,1)} %param.18) | copy-start | bytes 1572868
  9.6 38.8 %copy-start.8 = (f32[2048]{0:T(1024)S(1)}, f32[2048]{0:T(1024)}, u32[]{:S(2)}) copy-start(f32[2048]{0:T(1024)} %param.15) | copy-start | bytes 24580
  65.2 2.8 copy-start.5
  65.2 132.5 %copy-start.3 = (f32[2048]{0:T(1024)S(1)}, f32[2048]{0:T(1024)}, u32[]{:S(2)}) copy-start(f32[2048]{0:T(1024)} %param.20) | copy-start | bytes 24580
  265.1 3.5 copy-start.1
  277.8 7.0 %copy-start.6 = (f32[16,8]{0,1:T(8,128)S(1)}, f32[16,8]{0,1:T(8,128)}, u32[]{:S(2)}) copy-start(f32[16,8]{0,1:T(8,128)} %param.22) | copy-start | bytes 1540
  277.8 56.7 %all-to-all-start.1 = ((bf16[128,4,2048]{2,1,0:T(4,128)(2,1)}), bf16[128,4,2048]{2,1,0:T(4,128)(2,1)S(1)}, u32[]{:S(2)}, u32[]{:S(2)}) async-start(bf16[128,4,2048]{2,1,0:T(4,128)(2,1)} %reshape.86), calls=%async_computation.1 | async-start | bytes 4194304 | tf_op jit(solution)/shard_map/all_to_all | solution.py:122
  284.6 83.1 %all-reduce.5.cloned.1.call-start = ((), (), s32[]{:S(2)}) async-start(), calls=%async_computation.3 | async-start | bytes 262144 | tf_op jit(solution)/shard_map/psum | solution.py:135
Sparse Core Ops, SparseCore 0:
  68.2 128.4 all-reduce.2
  341.1 26.4 all-reduce.4
where the time goes:
time: 377 us; the launch traced here: 376 us
  waiting for transfers between devices  204 us (54%)
  blocking collectives  115 us (31%)
  matrix products  18 us (5%)
  between operations  13.6 us (4%)
  local copies, waits for them, and re-layouts  10.2 us (3%)
  other arithmetic  7.82 us (2%)
  starting transfers between devices  6.96 us (2%)
    psum x1, waiting for transfers between devices, per_device(): summed = lax.psum(partial_value, ('section', 'exp'))  128 us
    all_to_all x1, blocking collectives, per_device(): lax.all_to_all(doubled, ('seq', 'exp'), split_axis=0, concat_axis=0, tile...  63 us
    all_to_all x1, waiting for transfers between devices, per_device(): lax.all_to_all(jnp.dot(activated, down_halves[0], preferred_element_type=...  49.4 us
    psum x1, waiting for transfers between devices, per_device(): moe_total = lax.psum(moe_part, 'section')  26.6 us
    all_gather x1, blocking collectives, per_device(): piece_keys = lax.all_gather(key_rows, 'seq', axis=0, tiled=True)  20.5 us
    all_gather x1, blocking collectives, per_device(): piece_values = lax.all_gather(value_rows, 'seq', axis=0, tiled=True)  16.1 us
    all_gather x1, blocking collectives, per_device(): key_segs = lax.all_gather(seg_ids, 'seq', axis=0, tiled=True)  15.7 us
  transfers between devices with their start and end apart: 3, of which 3 were waited for; matrix products, arithmetic and copies ran while one was open for 0% of the time, Pallas kernels for 0%

commit v1 on v0

--- a/solution.py
+++ b/solution.py
@@ -6,6 +6,12 @@
 
 epsilon = 1e-05
 rope_base = 10000.0
+
+
+def tiled_gather(x, axis, dim):
+    length = lax.axis_size(axis)
+    repeats = [length if d == dim else 1 for d in range(x.ndim)]
+    return lax.all_to_all(jnp.tile(x, repeats), axis, split_axis=dim, concat_axis=dim, tiled=True)
 
 
 def rms_scale(rows, gain):
@@ -60,7 +66,7 @@
     value_rows = jnp.dot(normed, w_value, preferred_element_type=jnp.float32).astype(jnp.bfloat16)
     score_scale = 1.0 / math.sqrt(head_dim)
     run_max = jnp.full((tok_seq,), -1e30, jnp.float32)
-    piece_keys = lax.all_gather(key_rows, "seq", axis=0, tiled=True)
+    piece_keys = tiled_gather(key_rows, "seq", 0)
     piece_values = lax.all_gather(value_rows, "seq", axis=0, tiled=True)
     key_segs = lax.all_gather(seg_ids, "seq", axis=0, tiled=True)
     piece_rows = piece_keys.shape[0]

time: 377 us -> 365 us (0.968)
  blocking collectives: 115 us -> 98.1 us
  starting transfers between devices: 6.96 us -> 14.6 us
  waiting for transfers between devices: 204 us -> 199 us
    all_gather x1 -> x0, blocking collectives: 20.5 us -> none  [per_device(): piece_keys = lax.all_gather(key_rows, 'seq', axis=0, tiled=True)]
    all_to_all x0 -> x1, starting transfers between devices: none -> 7.57 us  [tiled_gather(): lax.all_to_all(jnp.tile(x, repeats), axis, split_axis=dim, concat_axis=di...]
    psum x1, waiting for transfers between devices: 128 us -> 123 us  [per_device(): summed = lax.psum(partial_value, ('section', 'exp'))]
  transfers between devices with their start and end apart: 3 -> 4, of which waited for: 3 -> 3; matrix products, arithmetic and copies ran while one was open for 0% -> 0% of each run, Pallas kernels for 0% -> 0%
where the time goes in v1:
time: 365 us; the launch traced here: 364 us
  waiting for transfers between devices  199 us (55%)
  blocking collectives  98.1 us (27%)
  matrix products  19.1 us (5%)
  starting transfers between devices  14.6 us (4%)
  between operations  13.7 us (4%)
  local copies, waits for them, and re-layouts  12 us (3%)
  other arithmetic  7.82 us (2%)
    psum x1, waiting for transfers between devices, per_device(): summed = lax.psum(partial_value, ('section', 'exp'))  123 us
    all_to_all x1, blocking collectives, per_device(): lax.all_to_all(doubled, ('seq', 'exp'), split_axis=0, concat_axis=0, tile...  63 us
    all_to_all x1, waiting for transfers between devices, per_device(): lax.all_to_all(jnp.dot(activated, down_halves[0], preferred_element_type=...  49.4 us
    psum x1, waiting for transfers between devices, per_device(): moe_total = lax.psum(moe_part, 'section')  26.6 us
    all_gather x1, blocking collectives, per_device(): key_segs = lax.all_gather(seg_ids, 'seq', axis=0, tiled=True)  18.6 us
    all_gather x1, blocking collectives, per_device(): piece_values = lax.all_gather(value_rows, 'seq', axis=0, tiled=True)  16.4 us
    all_to_all x1, starting transfers between devices, tiled_gather(): lax.all_to_all(jnp.tile(x, repeats), axis, split_axis=dim, concat_axis=di...  7.57 us
  transfers between devices with their start and end apart: 4, of which 3 were waited for; matrix products, arithmetic and copies ran while one was open for 0% of the time, Pallas kernels for 0%

profile of v1, /device:TPU:1, one launch (start us, length us, event | category | flops | bytes accessed | tf_op | source)
XLA Modules:
  0.0 364.1 jit_solution(2944089575382768795)
XLA Ops:
  6.5 1.3 fusion.4
  7.9 0.0 copy-start.5
  7.9 0.0 copy-start.2
  7.9 0.0 copy-start.8
  7.9 0.0 copy-start.9
  7.9 1.7 fusion.74
  9.6 1.6 fusion.76
  11.3 0.2 fusion.52
  11.5 0.1 copy.20
  11.6 0.9 tile.2
  12.5 7.6 %all-to-all-start = ((bf16[16,128,128]{2,1,0:T(8,128)(2,1)}), bf16[16,128,128]{2,1,0:T(8,128)(2,1)S(1)}, u32[]{:S(2)}, u32[]{:S(2)}) async-start(bf16[16,128,128]{2,1,0:T(8,128)(2,1)} %tile.2), calls=%async_computation | async-start | bytes 1048576 | tf_op jit(solution)/shard_map/all_to_all | solution.py:14
  20.1 0.0 all-reduce.3.cloned.1.call-start
  20.2 0.1 copy.22
  20.3 0.1 reshape.103
  20.4 18.6 %all-gather = s32[16,1,128]{2,1,0:T(1,128)S(1)} all-gather(s32[1,1,128]{2,1,0:T(1,128)S(1)} %bitcast.35), channel_id=1, replica_groups=mesh['section'=2,'seq'=16,'exp'=8] {'seq'}, dimensions={0}, use_global_device_ids=true | all-gather | bytes 8704 | tf_op jit(solution)/shard_map/all_gather | solution.py:71
  39.0 0.4 convolution_convert_fusion.2
  39.4 16.4 %all_gather.7 = bf16[2048,128]{1,0:T(8,128)(2,1)S(1)} all-gather(bf16[128,128]{1,0:T(8,128)(2,1)S(1)} %convolution_convert_fusion.2), channel_id=1, replica_groups=mesh['section'=2,'seq'=16,'exp'=8] {'seq'}, dimensions={0}, use_global_device_ids=true | all-gather | bytes 557056 | tf_op jit(solution)/shard_map/all_gather | solution.py:70
  55.8 0.8 copy-done.3
  56.6 1.6 fusion.78
  58.2 0.4 fusion.13
  58.6 2.8 fusion.3
  61.4 0.0 all-reduce.3.cloned.1.call-update
  61.4 0.1 fusion.42
  61.5 0.2 reduce_window_sum.11
  61.7 0.2 select_reduce_fusion
  61.9 122.9 %all-reduce.3.cloned.1.call-done = f32[128,2048]{1,0:T(8,128)} async-done(((f32[128,2048]{1,0:T(8,128)}), f32[128,2048]{1,0:T(8,128)}) %all-reduce.3.cloned.1.call-update) | async-done | bytes 1048592 | tf_op jit(solution)/shard_map/psum | solution.py:93
  184.7 1.0 fusion.35
  185.8 0.1 fusion.37
  185.9 0.5 convolution_convert_fusion.1
  186.4 0.4 broadcast_in_dim.19
  186.9 1.2 broadcast_in_dim.20
  188.1 63.0 %all_to_all.19 = bf16[128,4,2048]{2,1,0:T(4,128)(2,1)S(1)} all-to-all(bf16[128,4,2048]{2,1,0:T(4,128)(2,1)S(1)} %bitcast.30), channel_id=1, replica_groups=mesh['section'=2,'seq'=16,'exp'=8] {'seq','exp'}, dimensions={0} | all-to-all | bytes 4194304 | tf_op jit(solution)/shard_map/all_to_all | solution.py:123
  251.1 2.1 reshape.106
  253.2 3.5 fusion.10
  256.7 5.0 %convolution_convert_fusion = bf16[512,2048]{1,0:T(8,128)(2,1)} fusion(bf16[512,2048]{1,0:T(8,128)(2,1)S(1)} %copy-done.1, bf16[1,256,2048]{2,1,0:T(8,128)(2,1)S(1)} %copy-done, bf16[1,2048,256]{2,1,0:T(8,128)(2,1)} %param.24, f32[512,256]{1,0:T(8,128)} %fusion.10), kind=kOutput, calls=%fused_computation.1 | convolution fusion | flops 1075576832 | bytes 6815744 | tf_op jit(solution)/shard_map/dot_general | solution.py:129
  261.8 4.1 %reshape.107 = bf16[128,4,2048]{2,1,0:T(4,128)(2,1)} reshape(bf16[512,2048]{1,0:T(8,128)(2,1)} %convolution_convert_fusion) | data formatting | bytes 4194304 | tf_op jit(solution)/shard_map/reshape | solution.py:131
  265.9 6.7 %all-to-all-start.2 = ((bf16[128,4,2048]{2,1,0:T(4,128)(2,1)}), bf16[128,4,2048]{2,1,0:T(4,128)(2,1)S(1)}, u32[]{:S(2)}, u32[]{:S(2)}) async-start(bf16[128,4,2048]{2,1,0:T(4,128)(2,1)} %reshape.107), calls=%async_computation.2 | async-start | bytes 4194304 | tf_op jit(solution)/shard_map/all_to_all | solution.py:128
  272.6 0.2 all-reduce.5.cloned.1.call-start
  272.9 0.1 copy.21
  272.9 0.1 mul.147
  273.0 0.2 fusion.39
  273.2 49.4 %all-to-all-done.2 = bf16[128,4,2048]{2,1,0:T(4,128)(2,1)S(1)} async-done(((bf16[128,4,2048]{2,1,0:T(4,128)(2,1)}), bf16[128,4,2048]{2,1,0:T(4,128)(2,1)S(1)}, u32[]{:S(2)}, u32[]{:S(2)}) %all-to-all-start.2) | async-done | bytes 2097184 | tf_op jit(solution)/shard_map/all_to_all | solution.py:128
  322.6 2.7 convert_reduce_fusion
  325.3 2.0 reshape.108
  327.3 1.8 fusion.79
  329.0 0.0 all-reduce.5.cloned.1.call-update
  329.1 26.6 %all-reduce.5.cloned.1.call-done = f32[16,2048]{1,0:T(8,128)} async-done(((f32[16,2048]{1,0:T(8,128)}), f32[16,2048]{1,0:T(8,128)}) %all-reduce.5.cloned.1.call-update) | async-done | bytes 131088 | tf_op jit(solution)/shard_map/psum | solution.py:141
  355.7 1.5 fusion.38
  (25 shorter events, 0.1 us)
Async XLA Ops:
  6.5 250.2 %copy-start = (bf16[1,256,2048]{2,1,0:T(8,128)(2,1)S(1)}, bf16[1,256,2048]{2,1,0:T(8,128)(2,1)}, u32[]{:S(2)}) copy-start(bf16[1,256,2048]{2,1,0:T(8,128)(2,1)} %param.25) | copy-start | bytes 3145732
  7.9 12.3 %copy-start.6 = (s32[16,8]{0,1:T(8,128)S(1)}, s32[16,8]{0,1:T(8,128)}, u32[]{:S(2)}) copy-start(s32[16,8]{0,1:T(8,128)} %param.21) | copy-start | bytes 1540
  7.9 12.5 %copy-start.5 = (s32[128]{0:T(128)S(1)}, s32[128]{0:T(128)}, u32[]{:S(2)}) copy-start(s32[128]{0:T(128)} %param.14) | copy-start | bytes 1540
  7.9 31.1 %copy-start.2 = (bf16[128,2048]{1,0:T(8,128)(2,1)S(1)}, bf16[128,2048]{1,0:T(8,128)(2,1)}, u32[]{:S(2)}) copy-start(bf16[128,2048]{1,0:T(8,128)(2,1)} %param.13) | copy-start | bytes 1572868
  7.9 31.1 %copy-start.8 = (bf16[2048,128]{1,0:T(8,128)(2,1)S(1)}, bf16[2048,128]{1,0:T(8,128)(2,1)}, u32[]{:S(2)}) copy-start(bf16[2048,128]{1,0:T(8,128)(2,1)} %param.18) | copy-start | bytes 1572868
  7.9 31.1 %copy-start.9 = (f32[2048]{0:T(1024)S(1)}, f32[2048]{0:T(1024)}, u32[]{:S(2)}) copy-start(f32[2048]{0:T(1024)} %param.15) | copy-start | bytes 24580
  12.5 43.3 %all-to-all-start = ((bf16[16,128,128]{2,1,0:T(8,128)(2,1)}), bf16[16,128,128]{2,1,0:T(8,128)(2,1)S(1)}, u32[]{:S(2)}, u32[]{:S(2)}) async-start(bf16[16,128,128]{2,1,0:T(8,128)(2,1)} %tile.2), calls=%async_computation | async-start | bytes 1048576 | tf_op jit(solution)/shard_map/all_to_all | solution.py:14
  20.1 164.6 %all-reduce.3.cloned.1.call-start = ((), (), s32[]{:S(2)}) async-start(), calls=%async_computation.3 | async-start | bytes 2097152 | tf_op jit(solution)/shard_map/psum | solution.py:93
  55.8 0.8 copy-start.3
  58.6 127.2 %copy-start.4 = (f32[2048]{0:T(1024)S(1)}, f32[2048]{0:T(1024)}, u32[]{:S(2)}) copy-start(f32[2048]{0:T(1024)} %param.20) | copy-start | bytes 24580
  253.2 3.5 copy-start.1
  265.9 7.0 %copy-start.7 = (f32[16,8]{0,1:T(8,128)S(1)}, f32[16,8]{0,1:T(8,128)}, u32[]{:S(2)}) copy-start(f32[16,8]{0,1:T(8,128)} %param.22) | copy-start | bytes 1540
  265.9 56.7 %all-to-all-start.2 = ((bf16[128,4,2048]{2,1,0:T(4,128)(2,1)}), bf16[128,4,2048]{2,1,0:T(4,128)(2,1)S(1)}, u32[]{:S(2)}, u32[]{:S(2)}) async-start(bf16[128,4,2048]{2,1,0:T(4,128)(2,1)} %reshape.107), calls=%async_computation.2 | async-start | bytes 4194304 | tf_op jit(solution)/shard_map/all_to_all | solution.py:128
  272.6 83.1 %all-reduce.5.cloned.1.call-start = ((), (), s32[]{:S(2)}) async-start(), calls=%async_computation.4 | async-start | bytes 262144 | tf_op jit(solution)/shard_map/psum | solution.py:141
Sparse Core Ops, SparseCore 0:
  61.5 123.1 all-reduce.2
  329.2 26.4 all-reduce.4
